TPU v7x, 32 devices: a whole 2x2x4 slice. The times are simulated.
32 devices in a mesh: expert: 8 (over z, x), tensor: 4 (over y, core).
Axes of the slice: x: 2, y: 2, z: 4, core: 2. Of those that a mesh axis runs over, the one named last changes fastest.
Arguments:
- attn_heads: bfloat16 [1024, 4096], P('expert', 'tensor'), may hold values from -6 to 6
- out_proj: bfloat16 [4096, 4096], P('tensor', 'expert'), may hold values from -0.09375 to 0.09375
- residual: bfloat16 [1024, 4096], P('expert'), may hold values from -6 to 6
- norm_gain: bfloat16 [4096], replicated, may hold values from 0.099609375 to 1.8984375
- gate_proj: bfloat16 [16, 1536, 4096], P('expert', 'tensor'), may hold values from -0.09375 to 0.09375
- up_proj: bfloat16 [16, 1536, 4096], P('expert', 'tensor'), may hold values from -0.09375 to 0.09375
- down_proj: bfloat16 [16, 1536, 4096], P('expert', None, 'tensor'), may hold values from -0.15625 to 0.15625
- expert_ids: int32 [1024, 8], P('expert'), may hold values from 0 to 15, all different within a row; in each aligned block of 128 rows (0 to 127, 128 to 255, ...) at most 96 rows name the same one
- gate_scores: float32 [1024, 8], P('expert'), may hold values from 0.25 to 1
Outputs:
- layer_out: bfloat16 [1024, 4096], P('expert', 'tensor')
Inputs may be any that keep to these rules, and one draw needn't show every extreme that they name: `expert_ids`: each row names 8 different experts. Among the 128 rows of one device no expert is named by more than 96 rows, a bound that some block reaches.
All inputs are finite; a program needn't handle non-finite values.
Results may differ from a plain program's by a relative error of at most 0.0051.
Values may be sent and summed in bfloat16 or wider, within the bound.
No kernel may reach another device: no remote copies, remote signals or barrier semaphores. Data moves between devices by JAX's collectives and lax.ppermute only.
A program may use at most 128 MiB of HBM per device.

v0:
```python
import jax
import jax.numpy as jnp
from jax import lax
from jax.sharding import PartitionSpec as P

EPS = 1e-06


def on_device(
    attn_heads,
    out_proj,
    residual,
    norm_gain,
    gate_proj,
    up_proj,
    down_proj,
    expert_ids,
    gate_scores,
):
    tok_count = residual.shape[0]
    width = residual.shape[1]
    topk = expert_ids.shape[1]
    groups = lax.axis_size("expert")
    tensor_ways = lax.axis_size("tensor")
    exp_local = gate_proj.shape[0]
    experts_all = groups * exp_local
    slot_cap = 3 * tok_count * topk // (2 * experts_all)
    share = width // tensor_ways
    offset = lax.axis_index("tensor") * share
    partial_proj = jnp.dot(
        attn_heads,
        lax.all_gather(out_proj, "expert", axis=1, tiled=True),
        preferred_element_type=jnp.float32,
    )
    attn_part = lax.psum_scatter(partial_proj, "tensor", scatter_dimension=1, tiled=True)
    res_part = lax.dynamic_slice_in_dim(residual, offset, share, 1)
    state_part = (res_part.astype(jnp.float32) + attn_part).astype(jnp.bfloat16)
    state_f = state_part.astype(jnp.float32)
    squares = lax.psum(jnp.sum(state_f * state_f, axis=1), "tensor")
    gain_part = lax.dynamic_slice_in_dim(norm_gain, offset, share, 0)
    normed = (
        state_f * lax.rsqrt(squares / width + EPS)[:, None] * gain_part.astype(jnp.float32)
    ).astype(jnp.bfloat16)
    picks = expert_ids[:, :, None] == jnp.arange(experts_all, dtype=jnp.int32)[None, None, :]
    flag = jnp.sum(picks.astype(jnp.int32), axis=1)
    before = jnp.cumsum(flag, axis=0) - flag
    rank = jnp.sum(jnp.where(picks, before[:, None, :], 0), axis=2)
    slot = expert_ids * slot_cap + rank
    token_ids = jnp.arange(tok_count * topk, dtype=jnp.int32) // topk + 1
    owner = jnp.zeros((experts_all * slot_cap,), jnp.int32).at[slot.reshape(-1)].set(token_ids)
    rows = jnp.take(normed, jnp.maximum(owner - 1, 0), axis=0)
    rows = jnp.where((owner > 0)[:, None], rows, jnp.zeros((), jnp.bfloat16))
    send = rows.reshape(groups, exp_local, slot_cap, rows.shape[1])
    block = lax.all_gather(
        lax.all_to_all(send, "expert", split_axis=0, concat_axis=0, tiled=True),
        "tensor",
        axis=3,
        tiled=True,
    )
    count = block.shape[2]
    stacked = jnp.transpose(block, (1, 0, 2, 3)).reshape(exp_local, groups * count, width)
    gate = jnp.einsum("erd,efd->erf", stacked, gate_proj, preferred_element_type=jnp.float32)
    upper = jnp.einsum("erd,efd->erf", stacked, up_proj, preferred_element_type=jnp.float32)
    act = (jax.nn.silu(gate) * upper).astype(jnp.bfloat16)
    whole_act = lax.all_gather(act, "tensor", axis=2, tiled=True)
    result = jnp.einsum(
        "erf,efd->erd", whole_act, down_proj, preferred_element_type=jnp.float32
    ).astype(jnp.bfloat16)
    result = jnp.transpose(result.reshape(exp_local, groups, count, share), (1, 0, 2, 3))
    back = lax.all_to_all(result, "expert", split_axis=0, concat_axis=0, tiled=True)
    flat = back.reshape(experts_all * slot_cap, share)
    picked = jnp.take(flat, slot.reshape(-1), axis=0).reshape(tok_count, topk, share)
    weights = gate_scores / jnp.sum(gate_scores, axis=1, keepdims=True)
    mixture = jnp.einsum("tk,tkd->td", weights, picked.astype(jnp.float32))
    return (state_part.astype(jnp.float32) + mixture).astype(jnp.bfloat16)


def solution(mesh):
    in_specs = (
        P("expert", "tensor"),
        P("tensor", "expert"),
        P("expert", None),
        P(),
        P("expert", "tensor", None),
        P("expert", "tensor", None),
        P("expert", None, "tensor"),
        P("expert", None),
        P("expert", None),
    )
    out_specs = P("expert", "tensor")
    return jax.shard_map(
        on_device, mesh=mesh, in_specs=in_specs, out_specs=out_specs, check_vma=False
    )
```

profile of v0, /device:TPU:0, one launch (start us, length us, event | category | flops | bytes accessed | tf_op | source)
XLA Modules:
  0.0 507.4 jit_solution(3773535396827234200)
XLA Ops:
  6.5 0.0 copy-start
  6.5 0.0 all-gather.4.cloned.1.call-start
  6.5 0.7 all-gather.4.cloned.1.call-update
  7.3 0.0 copy-start.4
  7.3 0.0 reduce-scatter.2.cloned.1.call-start
  7.3 130.2 %all-gather.4.cloned.1.call-done = bf16[1024,4096]{1,0:T(8,128)(2,1)} async-done(((bf16[1024,512]{1,0:T(8,128)(2,1)}), bf16[1024,4096]{1,0:T(8,128)(2,1)}) %all-gather.4.cloned.1.call-update) | async-done | bytes 8388624 | tf_op jit(solution)/shard_map/all_gather | solution.py:32
  137.5 0.0 copy-done
  137.5 6.0 %fusion.14 = f32[128,4096]{1,0:T(8,128)} fusion(bf16[128,1024]{1,0:T(8,128)(2,1)S(1)} %copy-done, bf16[1024,4096]{1,0:T(8,128)(2,1)} %all-gather.4.cloned.1.call-done), kind=kOutput, calls=%fused_computation.45 | convolution fusion | flops 1073741824 | bytes 10747904 | tf_op jit(solution)/shard_map/dot_general | solution.py:30
  143.5 0.0 reduce-scatter.2.cloned.1.call-update
  143.5 0.0 all-gather.6.cloned.1.call-start
  143.6 0.0 copy-done.4
  143.6 0.1 copy.26
  143.7 0.2 reduce_window_sum.11
  143.9 0.1 copy.28
  144.0 0.1 copy.30
  144.1 0.1 reshape.84
  144.3 4.3 scatter_custom_fusion
  148.6 0.1 broadcast_in_dim.61
  148.7 0.1 broadcast_in_dim.63
  148.8 0.7 dynamic-slice_convert_fusion
  149.5 23.8 %reduce-scatter.2.cloned.1.call-done = f32[128,1024]{1,0:T(8,128)} async-done(((f32[128,4096]{1,0:T(8,128)}), f32[128,1024]{1,0:T(8,128)}) %reduce-scatter.2.cloned.1.call-update) | async-done | bytes 524304 | tf_op jit(solution)/shard_map/reduce_scatter | solution.py:35
  173.3 1.3 fusion.3
  174.6 0.0 copy-start.2
  174.6 5.8 %psum.7 = f32[128]{0:T(128)S(1)} all-reduce(f32[128]{0:T(128)S(1)} %get-tuple-element.7), channel_id=1, replica_groups=mesh['expert'=8,'tensor'=4] {'tensor'}, use_global_device_ids=true, to_apply=%region_7.8 | all-reduce | flops 128 | bytes 1024 | tf_op jit(solution)/shard_map/psum | solution.py:39
  180.3 0.0 copy-done.2
  180.4 0.1 fusion.5
  180.5 5.1 gather_fusion
  185.6 0.6 select_select_fusion
  186.2 76.2 %all_to_all.10 = bf16[8,2,96,1024]{3,2,1,0:T(8,128)(2,1)} all-to-all(bf16[8,2,96,1024]{3,2,1,0:T(8,128)(2,1)S(1)} %select_select_fusion), channel_id=1, replica_groups=mesh['expert'=8,'tensor'=4] {'expert'}, dimensions={0} | all-to-all | bytes 6291456 | tf_op jit(solution)/shard_map/all_to_all | solution.py:55
  262.4 0.0 slice-start
  262.4 0.0 all-gather.6.cloned.1.call-update
  262.5 0.2 all-gather.8.cloned.1.call-start
  262.7 80.0 %all-gather.6.cloned.1.call-done = bf16[8,2,96,4096]{3,2,1,0:T(8,128)(2,1)} async-done(((bf16[8,2,96,1024]{3,2,1,0:T(8,128)(2,1)}), bf16[8,2,96,4096]{3,2,1,0:T(8,128)(2,1)}) %all-gather.6.cloned.1.call-update) | async-done | bytes 12582928 | tf_op jit(solution)/shard_map/all_gather | solution.py:54
  342.7 0.0 slice-start.1
  342.7 6.6 %copy.31 = bf16[2,8,96,4096]{3,2,1,0:T(8,128)(2,1)S(1)} copy(bf16[2,8,96,4096]{3,2,0,1:T(8,128)(2,1)} %bitcast.26) | data formatting | bytes 25165824 | tf_op jit(solution)/shard_map/transpose | solution.py:61
  349.3 0.0 slice-done
  349.3 0.0 slice-done.1
  349.3 8.1 %fusion.15 = f32[2,768,384]{2,1,0:T(8,128)} fusion(bf16[2,768,4096]{2,1,0:T(8,128)(2,1)S(1)} %bitcast.27, bf16[2,384,4096]{2,1,0:T(8,128)(2,1)S(1)} %bitcast.35), kind=kOutput, calls=%fused_computation.46 | convolution fusion | flops 4831838208 | bytes 21233664 | tf_op jit(solution)/shard_map/erd,efd->erf/dot_general | solution.py:62
  357.4 10.0 %multiply_convert_fusion = bf16[2,768,384]{2,1,0:T(8,128)(2,1)} fusion(f32[2,768,384]{2,1,0:T(8,128)} %fusion.15, bf16[2,768,4096]{2,1,0:T(8,128)(2,1)S(1)} %bitcast.28, bf16[2,384,4096]{2,1,0:T(8,128)(2,1)} %param.14), kind=kOutput, calls=%fused_computation.5 | convolution fusion | flops 4835377152 | bytes 22413312 | tf_op jit(solution)/shard_map/erd,efd->erf/dot_general | solution.py:63
  367.4 0.0 all-gather.8.cloned.1.call-update
  367.5 37.6 %all-gather.8.cloned.1.call-done = bf16[2,768,1536]{2,1,0:T(8,128)(2,1)} async-done(((bf16[2,768,384]{2,1,0:T(8,128)(2,1)}), bf16[2,768,1536]{2,1,0:T(8,128)(2,1)}) %all-gather.8.cloned.1.call-update) | async-done | bytes 4718608 | tf_op jit(solution)/shard_map/all_gather | solution.py:65
  405.0 8.6 %convolution_convert_fusion = bf16[2,768,1024]{2,1,0:T(8,128)(2,1)S(1)} fusion(bf16[2,768,1536]{2,1,0:T(8,128)(2,1)} %all-gather.8.cloned.1.call-done, bf16[2,1536,1024]{2,1,0:T(8,128)(2,1)} %param.15), kind=kOutput, calls=%fused_computation.6 | convolution fusion | flops 4833411072 | bytes 14155776 | tf_op jit(solution)/shard_map/erf,efd->erd/dot_general | solution.py:66
  413.6 1.9 copy.37
  415.5 0.0 copy-start.5
  415.5 5.6 %all-to-all-start.1 = ((bf16[8,2,96,1024]{3,2,1,0:T(8,128)(2,1)}), bf16[8,2,96,1024]{3,2,1,0:T(8,128)(2,1)S(1)}, u32[]{:S(2)}, u32[]{:S(2)}) async-start(bf16[8,2,96,1024]{3,2,1,0:T(8,128)(2,1)} %bitcast.29), calls=%async_computation.2 | async-start | bytes 6291456 | tf_op jit(solution)/shard_map/all_to_all | solution.py:70
  421.2 0.1 copy.29
  421.3 0.0 copy-done.5
  421.3 0.1 copy.33
  421.5 70.8 %all-to-all-done.1 = bf16[8,2,96,1024]{3,2,1,0:T(8,128)(2,1)S(1)} async-done(((bf16[8,2,96,1024]{3,2,1,0:T(8,128)(2,1)}), bf16[8,2,96,1024]{3,2,1,0:T(8,128)(2,1)S(1)}, u32[]{:S(2)}, u32[]{:S(2)}) %all-to-all-start.1) | async-done | bytes 3145760 | tf_op jit(solution)/shard_map/all_to_all | solution.py:70
  492.3 0.0 copy-start.1
  492.3 5.3 %gather_fusion.1 = bf16[1024,1024]{1,0:T(8,128)(2,1)} fusion(bf16[1536,1024]{1,0:T(8,128)(2,1)S(1)} %bitcast.25, s32[1024]{0:T(1024)S(1)} %broadcast_clamp_fusion), kind=kCustom, calls=%fused_computation.1 | custom fusion | bytes 4198400 | tf_op jit(solution)/shard_map/jit(_take)/gather | solution.py:72
  497.6 0.0 copy-start.3
  497.6 2.4 fusion
  500.1 0.0 copy-done.3
  500.1 0.8 fusion.6
  500.9 0.0 copy-done.1
  (14 shorter events, 0.1 us)
Async XLA Ops:
  6.5 131.0 %copy-start = (bf16[128,1024]{1,0:T(8,128)(2,1)S(1)}, bf16[128,1024]{1,0:T(8,128)(2,1)}, u32[]{:S(2)}) copy-start(bf16[128,1024]{1,0:T(8,128)(2,1)} %param.9) | copy-start | bytes 786436
  6.5 131.0 %all-gather.4.cloned.1.call-start = ((), (), s32[]{:S(2)}) async-start(), calls=%async_computation.3 | async-start | bytes 9437184 | tf_op jit(solution)/shard_map/all_gather | solution.py:32
  7.3 136.3 %copy-start.4 = (s32[128,8]{0,1:T(8,128)S(1)}, s32[128,8]{0,1:T(8,128)}, u32[]{:S(2)}) copy-start(s32[128,8]{0,1:T(8,128)} %param.16) | copy-start | bytes 12292
  7.3 166.0 %reduce-scatter.2.cloned.1.call-start = ((), (), s32[]{:S(2)}) async-start(), calls=%async_computation.4 | async-start | bytes 2621440 | tf_op jit(solution)/shard_map/reduce_scatter | solution.py:35
  143.5 199.1 %all-gather.6.cloned.1.call-start = ((), (), s32[]{:S(2)}) async-start(), calls=%async_computation.5 | async-start | bytes 15728640 | tf_op jit(solution)/shard_map/all_gather | solution.py:54
  174.6 5.8 %copy-start.2 = (bf16[128,1024]{1,0:T(8,128)(2,1)}, bf16[128,1024]{1,0:T(8,128)(2,1)S(1)}, u32[]{:S(2)}) copy-start(bf16[128,1024]{1,0:T(8,128)(2,1)S(1)} %get-tuple-element.8) | copy-start | bytes 786436
  262.4 86.8 %slice-start = ((s8[6291456]{0:T(1024)(128)(4,1)}), s8[2097152]{0:T(1024)(128)(4,1)S(1)}, s32[]{:S(2)}) async-start(s8[6291456]{0:T(1024)(128)(4,1)} %bitcast.34), calls=%async_computation.7 | async-start | bytes 4194304
  262.5 142.5 %all-gather.8.cloned.1.call-start = ((), (), s32[]{:S(2)}) async-start(), calls=%async_computation.6 | async-start | bytes 5898240 | tf_op jit(solution)/shard_map/all_gather | solution.py:65
  342.7 6.6 %slice-start.1 = ((s8[6291456]{0:T(1024)(128)(4,1)}), s8[4194304]{0:T(1024)(128)(4,1)S(1)}, s32[]{:S(2)}) async-start(s8[6291456]{0:T(1024)(128)(4,1)} %bitcast.34), calls=%async_computation.8 | async-start | bytes 8388608
  415.5 5.8 %copy-start.5 = (f32[128,8]{0,1:T(8,128)S(1)}, f32[128,8]{0,1:T(8,128)}, u32[]{:S(2)}) copy-start(f32[128,8]{0,1:T(8,128)} %param.17) | copy-start | bytes 12292
  415.5 76.8 %all-to-all-start.1 = ((bf16[8,2,96,1024]{3,2,1,0:T(8,128)(2,1)}), bf16[8,2,96,1024]{3,2,1,0:T(8,128)(2,1)S(1)}, u32[]{:S(2)}, u32[]{:S(2)}) async-start(bf16[8,2,96,1024]{3,2,1,0:T(8,128)(2,1)} %bitcast.29), calls=%async_computation.2 | async-start | bytes 6291456 | tf_op jit(solution)/shard_map/all_to_all | solution.py:70
  492.3 8.6 %copy-start.1 = (bf16[128,1024]{1,0:T(8,128)(2,1)S(1)}, bf16[128,1024]{1,0:T(8,128)(2,1)}, u32[]{:S(2)}) copy-start(bf16[128,1024]{1,0:T(8,128)(2,1)} %param.9) | copy-start | bytes 786436
  497.6 2.4 copy-start.3
Sparse Core Ops, SparseCore 0:
  9.4 128.0 all-gather.3
  143.7 29.5 reduce-scatter.1
  262.6 80.0 all-gather.5
  367.6 37.3 all-gather.7
where the time goes:
time: 508 us; the launch traced here: 507 us
  waiting for transfers between devices  343 us (68%)
  blocking collectives  82 us (16%)
  matrix products  35.1 us (7%)
  local copies, waits for them, and re-layouts  24.1 us (5%)
  between operations  13.3 us (3%)
  starting transfers between devices  5.95 us (1%)
    all_gather x1, waiting for transfers between devices, on_device(): lax.all_gather(out_proj, 'expert', axis=1, tiled=True)  130 us
    all_gather x1, waiting for transfers between devices, on_device(): lax.all_gather(lax.all_to_all(send, 'expert', split_axis=0, concat_axis=0...  80 us
    all_to_all x1, blocking collectives, on_device(): lax.all_to_all(send, 'expert', split_axis=0, concat_axis=0, tiled=True)  76.2 us
    all_to_all x1, waiting for transfers between devices, on_device(): lax.all_to_all(result, 'expert', split_axis=0, concat_axis=0, tiled=True)  70.8 us
    all_gather x1, waiting for transfers between devices, on_device(): whole_act = lax.all_gather(act, 'tensor', axis=2, tiled=True)  37.6 us
    reduce_scatter x1, waiting for transfers between devices, on_device(): lax.psum_scatter(partial_proj, 'tensor', scatter_dimension=1, tiled=True)  23.8 us
  transfers between devices with their start and end apart: 5, of which 5 were waited for; matrix products, arithmetic and copies ran while one was open for 1% of the time, Pallas kernels for 0%

commit v1 on v0

--- a/solution.py
+++ b/solution.py
@@ -62,7 +62,14 @@
     gate = jnp.einsum("erd,efd->erf", stacked, gate_proj, preferred_element_type=jnp.float32)
     upper = jnp.einsum("erd,efd->erf", stacked, up_proj, preferred_element_type=jnp.float32)
     act = (jax.nn.silu(gate) * upper).astype(jnp.bfloat16)
-    whole_act = lax.all_gather(act, "tensor", axis=2, tiled=True)
+    ring = [act]
+    for hop in range(3):
+        ring.append(lax.ppermute(ring[-1], "tensor", [(dev, (dev + 1) % 4) for dev in range(4)]))
+    whole_act = jnp.roll(
+        jnp.concatenate(ring[::-1], axis=2),
+        (lax.axis_index("tensor") + 1) * ring[0].shape[2],
+        axis=2,
+    )
     result = jnp.einsum(
         "erf,efd->erd", whole_act, down_proj, preferred_element_type=jnp.float32
     ).astype(jnp.bfloat16)

time: 508 us -> 535 us (1.053)
  local copies, waits for them, and re-layouts: 24.1 us -> 34.2 us
  matrix products: 35.1 us -> 43.5 us
  waiting for transfers between devices: 343 us -> 351 us
    ppermute x0 -> x3, waiting for transfers between devices: none -> 47 us  [on_device(): lax.ppermute(ring[-1], 'tensor', [(dev, (dev + 1) % 4) for dev in range(4)])]
    all_gather x1 -> x0, waiting for transfers between devices: 37.6 us -> none  [on_device(): whole_act = lax.all_gather(act, 'tensor', axis=2, tiled=True)]
    dot_general x1, matrix products: 8.07 us -> 15 us  [on_device(): jnp.einsum('erd,efd->erf', stacked, gate_proj, preferred_element_type=jnp...]
    unnamed x16 -> x21, local copies, waits for them, and re-layouts: 0.03 us -> 5.96 us
  transfers between devices with their start and end apart: 5 -> 7, of which waited for: 5 -> 7; matrix products, arithmetic and copies ran while one was open for 1% -> 1% of each run, Pallas kernels for 0% -> 0%
where the time goes in v1:
time: 535 us
  waiting for transfers between devices  351 us (66%)
  blocking collectives  82 us (15%)
  matrix products  43.5 us (8%)
  local copies, waits for them, and re-layouts  34.2 us (6%)
  between operations  13.3 us (2%)
  starting transfers between devices  6.05 us (1%)
    all_gather x1, waiting for transfers between devices, on_device(): lax.all_gather(out_proj, 'expert', axis=1, tiled=True)  130 us
    all_gather x1, waiting for transfers between devices, on_device(): lax.all_gather(lax.all_to_all(send, 'expert', split_axis=0, concat_axis=0...  80.2 us
    all_to_all x1, blocking collectives, on_device(): lax.all_to_all(send, 'expert', split_axis=0, concat_axis=0, tiled=True)  76.2 us
    all_to_all x1, waiting for transfers between devices, on_device(): lax.all_to_all(result, 'expert', split_axis=0, concat_axis=0, tiled=True)  68.8 us
    ppermute x3, waiting for transfers between devices, on_device(): lax.ppermute(ring[-1], 'tensor', [(dev, (dev + 1) % 4) for dev in range(4)])  47 us
    reduce_scatter x1, waiting for transfers between devices, on_device(): lax.psum_scatter(partial_proj, 'tensor', scatter_dimension=1, tiled=True)  23.8 us
    dot_general x1, matrix products, on_device(): jnp.einsum('erd,efd->erf', stacked, gate_proj, preferred_element_type=jnp...  15 us
    dot_general x1, matrix products, on_device(): jnp.einsum('erd,efd->erf', stacked, up_proj, preferred_element_type=jnp.f...  14.5 us
  transfers between devices with their start and end apart: 7, of which 7 were waited for; matrix products, arithmetic and copies ran while one was open for 1% of the time, Pallas kernels for 0%

profile of v1, /device:TPU:0, one launch (start us, length us, event | category | flops | bytes accessed | tf_op | source)
XLA Modules:
  0.0 534.7 jit_solution(15912184411036667015)
XLA Ops:
  6.5 0.0 copy-start
  6.5 0.0 all-gather.3.cloned.1.call-start
  6.5 0.7 all-gather.3.cloned.1.call-update
  7.3 0.0 copy-start.3
  7.3 0.0 reduce-scatter.2.cloned.1.call-start
  7.3 130.2 %all-gather.3.cloned.1.call-done = bf16[1024,4096]{1,0:T(8,128)(2,1)} async-done(((bf16[1024,512]{1,0:T(8,128)(2,1)}), bf16[1024,4096]{1,0:T(8,128)(2,1)}) %all-gather.3.cloned.1.call-update) | async-done | bytes 8388624 | tf_op jit(solution)/shard_map/all_gather | solution.py:32
  137.5 0.0 copy-done
  137.5 6.0 %fusion.20 = f32[128,4096]{1,0:T(8,128)} fusion(bf16[128,1024]{1,0:T(8,128)(2,1)S(1)} %copy-done, bf16[1024,4096]{1,0:T(8,128)(2,1)} %all-gather.3.cloned.1.call-done), kind=kOutput, calls=%fused_computation.56 | convolution fusion | flops 1073741824 | bytes 10747904 | tf_op jit(solution)/shard_map/dot_general | solution.py:30
  143.5 0.0 reduce-scatter.2.cloned.1.call-update
  143.6 0.0 all-gather.5.cloned.1.call-start
  143.6 0.0 copy-done.3
  143.6 0.1 copy.29
  143.7 0.2 reduce_window_sum.11
  143.9 0.1 copy.31
  144.0 0.1 copy.33
  144.1 0.1 reshape.84
  144.3 4.3 scatter_custom_fusion
  148.6 0.1 broadcast_in_dim.61
  148.7 0.1 broadcast_in_dim.63
  148.8 0.7 dynamic-slice_convert_fusion
  149.5 23.8 %reduce-scatter.2.cloned.1.call-done = f32[128,1024]{1,0:T(8,128)} async-done(((f32[128,4096]{1,0:T(8,128)}), f32[128,1024]{1,0:T(8,128)}) %reduce-scatter.2.cloned.1.call-update) | async-done | bytes 524304 | tf_op jit(solution)/shard_map/reduce_scatter | solution.py:35
  173.3 1.3 fusion.8
  174.6 0.0 copy-start.2
  174.6 5.8 %psum.7 = f32[128]{0:T(128)S(1)} all-reduce(f32[128]{0:T(128)S(1)} %get-tuple-element.7), channel_id=1, replica_groups=mesh['expert'=8,'tensor'=4] {'tensor'}, use_global_device_ids=true, to_apply=%region_7.8 | all-reduce | flops 128 | bytes 1024 | tf_op jit(solution)/shard_map/psum | solution.py:39
  180.4 0.0 copy-done.2
  180.4 0.1 fusion.10
  180.5 5.1 gather_fusion
  185.6 0.6 select_select_fusion
  186.2 76.2 %all_to_all.10 = bf16[8,2,96,1024]{3,2,1,0:T(8,128)(2,1)} all-to-all(bf16[8,2,96,1024]{3,2,1,0:T(8,128)(2,1)S(1)} %select_select_fusion), channel_id=1, replica_groups=mesh['expert'=8,'tensor'=4] {'expert'}, dimensions={0} | all-to-all | bytes 6291456 | tf_op jit(solution)/shard_map/all_to_all | solution.py:55
  262.4 0.0 all-gather.5.cloned.1.call-update
  262.5 80.2 %all-gather.5.cloned.1.call-done = bf16[8,2,96,4096]{3,2,1,0:T(8,128)(2,1)} async-done(((bf16[8,2,96,1024]{3,2,1,0:T(8,128)(2,1)}), bf16[8,2,96,4096]{3,2,1,0:T(8,128)(2,1)}) %all-gather.5.cloned.1.call-update) | async-done | bytes 12582928 | tf_op jit(solution)/shard_map/all_gather | solution.py:54
  342.7 10.7 %copy.34 = bf16[2,8,96,4096]{3,2,1,0:T(8,128)(2,1)} copy(bf16[2,8,96,4096]{3,2,0,1:T(8,128)(2,1)} %bitcast.25) | data formatting | bytes 25165824 | tf_op jit(solution)/shard_map/transpose | solution.py:61
  353.3 15.0 %fusion.21 = f32[2,768,384]{1,2,0:T(8,128)} fusion(bf16[2,768,4096]{2,1,0:T(8,128)(2,1)} %bitcast.26, bf16[2,384,4096]{2,1,0:T(8,128)(2,1)} %param.13), kind=kOutput, calls=%fused_computation.57 | convolution fusion | flops 4831838208 | bytes 21233664 | tf_op jit(solution)/shard_map/erd,efd->erf/dot_general | solution.py:62
  368.4 14.5 %multiply_convert_fusion = bf16[2,768,384]{1,2,0:T(8,128)(2,1)S(1)} fusion(f32[2,768,384]{1,2,0:T(8,128)} %fusion.21, bf16[2,768,4096]{2,1,0:T(8,128)(2,1)} %bitcast.27, bf16[2,384,4096]{2,1,0:T(8,128)(2,1)} %param.14), kind=kOutput, calls=%fused_computation.7 | convolution fusion | flops 4835377152 | bytes 22413312 | tf_op jit(solution)/shard_map/erd,efd->erf/dot_general | solution.py:63
  382.9 0.3 collective-permute-start
  383.2 15.4 %collective-permute-done = bf16[2,768,384]{1,2,0:T(8,128)(2,1)S(1)} collective-permute-done((bf16[2,768,384]{1,2,0:T(8,128)(2,1)S(1)}, bf16[2,768,384]{1,2,0:T(8,128)(2,1)S(1)}, u32[]{:S(2)}, u32[]{:S(2)}) %collective-permute-start) | collective-permute-done | bytes 1179680 | tf_op jit(solution)/shard_map/ppermute | solution.py:67
  398.6 0.0 collective-permute-start.1
  398.6 15.7 %collective-permute-done.1 = bf16[2,768,384]{1,2,0:T(8,128)(2,1)} collective-permute-done((bf16[2,768,384]{1,2,0:T(8,128)(2,1)S(1)}, bf16[2,768,384]{1,2,0:T(8,128)(2,1)}, u32[]{:S(2)}, u32[]{:S(2)}) %collective-permute-start.1) | collective-permute-done | bytes 1179680 | tf_op jit(solution)/shard_map/ppermute | solution.py:67
  414.3 0.0 collective-permute-start.2
  414.3 15.9 %collective-permute-done.2 = bf16[2,768,384]{1,2,0:T(8,128)(2,1)} collective-permute-done((bf16[2,768,384]{1,2,0:T(8,128)(2,1)}, bf16[2,768,384]{1,2,0:T(8,128)(2,1)}, u32[]{:S(2)}, u32[]{:S(2)}) %collective-permute-start.2) | collective-permute-done | bytes 1179680 | tf_op jit(solution)/shard_map/ppermute | solution.py:67
  430.3 1.3 constant_dynamic-update-slice_fusion.7
  431.6 0.0 slice-start
  431.6 1.5 constant_dynamic-update-slice_fusion.6
  433.1 0.1 constant_dynamic-update-slice_fusion.5
  433.2 0.1 constant_dynamic-update-slice_fusion.4
  433.3 0.0 slice-start.1
  433.3 1.5 constant_dynamic-update-slice_fusion.3
  434.8 1.3 constant_dynamic-update-slice_fusion.2
  436.2 0.1 constant_dynamic-update-slice_fusion.1
  436.3 0.1 constant_dynamic-update-slice_fusion
  436.3 0.0 slice-done
  436.3 0.0 slice-done.1
  436.4 5.6 %fusion.2 = bf16[2,768,1024]{2,1,0:T(8,128)(2,1)S(1)} fusion(bf16[2,1536,1024]{2,1,0:T(8,128)(2,1)S(1)} %bitcast.34, bf16[2,768,3072]{1,2,0:T(8,128)(2,1)S(1)} %constant_dynamic-update-slice_fusion, s32[]{:T(128)S(6)} %select_n.69), kind=kOutput, calls=%fused_computation.8 | convolution fusion | flops 4833411072 | bytes 14155780 | tf_op jit(solution)/shard_map/erf,efd->erd/dot_general | solution.py:73
  441.9 2.0 copy.42
  443.9 0.0 copy-start.4
  443.9 5.6 %all-to-all-start.1 = ((bf16[8,2,96,1024]{3,2,1,0:T(8,128)(2,1)}), bf16[8,2,96,1024]{3,2,1,0:T(8,128)(2,1)S(1)}, u32[]{:S(2)}, u32[]{:S(2)}) async-start(bf16[8,2,96,1024]{3,2,1,0:T(8,128)(2,1)} %bitcast.28), calls=%async_computation.2 | async-start | bytes 6291456 | tf_op jit(solution)/shard_map/all_to_all | solution.py:77
  449.6 0.1 copy.32
  449.7 0.0 copy-done.4
  449.7 0.1 copy.38
  449.9 68.8 %all-to-all-done.1 = bf16[8,2,96,1024]{3,2,1,0:T(8,128)(2,1)S(1)} async-done(((bf16[8,2,96,1024]{3,2,1,0:T(8,128)(2,1)}), bf16[8,2,96,1024]{3,2,1,0:T(8,128)(2,1)S(1)}, u32[]{:S(2)}, u32[]{:S(2)}) %all-to-all-start.1) | async-done | bytes 3145760 | tf_op jit(solution)/shard_map/all_to_all | solution.py:77
  518.6 5.3 gather_fusion.1
  524.0 2.4 fusion.5
  526.4 1.8 fusion.11
  528.1 0.0 copy-done.1
  (15 shorter events, 0.1 us)
Async XLA Ops:
  6.5 131.0 %copy-start = (bf16[128,1024]{1,0:T(8,128)(2,1)S(1)}, bf16[128,1024]{1,0:T(8,128)(2,1)}, u32[]{:S(2)}) copy-start(bf16[128,1024]{1,0:T(8,128)(2,1)} %param.9) | copy-start | bytes 786436
  6.5 131.0 %all-gather.3.cloned.1.call-start = ((), (), s32[]{:S(2)}) async-start(), calls=%async_computation.3 | async-start | bytes 9437184 | tf_op jit(solution)/shard_map/all_gather | solution.py:32
  7.3 136.4 %copy-start.3 = (s32[128,8]{0,1:T(8,128)S(1)}, s32[128,8]{0,1:T(8,128)}, u32[]{:S(2)}) copy-start(s32[128,8]{0,1:T(8,128)} %param.16) | copy-start | bytes 12292
  7.3 166.0 %reduce-scatter.2.cloned.1.call-start = ((), (), s32[]{:S(2)}) async-start(), calls=%async_computation.4 | async-start | bytes 2621440 | tf_op jit(solution)/shard_map/reduce_scatter | solution.py:35
  143.6 199.1 %all-gather.5.cloned.1.call-start = ((), (), s32[]{:S(2)}) async-start(), calls=%async_computation.5 | async-start | bytes 15728640 | tf_op jit(solution)/shard_map/all_gather | solution.py:54
  174.6 5.8 %copy-start.2 = (bf16[128,1024]{1,0:T(8,128)(2,1)}, bf16[128,1024]{1,0:T(8,128)(2,1)S(1)}, u32[]{:S(2)}) copy-start(bf16[128,1024]{1,0:T(8,128)(2,1)S(1)} %get-tuple-element.8) | copy-start | bytes 786436
  382.9 15.7 %collective-permute-start = (bf16[2,768,384]{1,2,0:T(8,128)(2,1)S(1)}, bf16[2,768,384]{1,2,0:T(8,128)(2,1)S(1)}, u32[]{:S(2)}, u32[]{:S(2)}) collective-permute-start(bf16[2,768,384]{1,2,0:T(8,128)(2,1)S(1)} %multiply_convert_fusion), channel_id=1, source_target_pairs={{0,1},{1,2},{2,3},{3,0},{4,5},{5,6},{6,7},{7,4},{8,9},{9,10},{10,1... | collective-permute-start | bytes 3538952 | tf_op jit(solution)/shard_map/ppermute | solution.py:67
  398.6 15.7 %collective-permute-start.1 = (bf16[2,768,384]{1,2,0:T(8,128)(2,1)S(1)}, bf16[2,768,384]{1,2,0:T(8,128)(2,1)}, u32[]{:S(2)}, u32[]{:S(2)}) collective-permute-start(bf16[2,768,384]{1,2,0:T(8,128)(2,1)S(1)} %collective-permute-done), channel_id=1, source_target_pairs={{0,1},{1,2},{2,3},{3,0},{4,5},{5,6},{6,7},{7,4},{8,9},{9,10},{10,1... | collective-permute-start | bytes 3538952 | tf_op jit(solution)/shard_map/ppermute | solution.py:67
  414.3 15.9 %collective-permute-start.2 = (bf16[2,768,384]{1,2,0:T(8,128)(2,1)}, bf16[2,768,384]{1,2,0:T(8,128)(2,1)}, u32[]{:S(2)}, u32[]{:S(2)}) collective-permute-start(bf16[2,768,384]{1,2,0:T(8,128)(2,1)} %collective-permute-done.1), channel_id=1, source_target_pairs={{0,1},{1,2},{2,3},{3,0},{4,5},{5,6},{6,7},{7,4},{8,9},{9,10},{10,1... | collective-permute-start | bytes 3538952 | tf_op jit(solution)/shard_map/ppermute | solution.py:67
  431.6 4.7 slice-start
  433.3 3.1 slice-start.1
  443.9 5.8 %copy-start.4 = (f32[128,8]{0,1:T(8,128)S(1)}, f32[128,8]{0,1:T(8,128)}, u32[]{:S(2)}) copy-start(f32[128,8]{0,1:T(8,128)} %param.17) | copy-start | bytes 12292
  443.9 74.7 %all-to-all-start.1 = ((bf16[8,2,96,1024]{3,2,1,0:T(8,128)(2,1)}), bf16[8,2,96,1024]{3,2,1,0:T(8,128)(2,1)S(1)}, u32[]{:S(2)}, u32[]{:S(2)}) async-start(bf16[8,2,96,1024]{3,2,1,0:T(8,128)(2,1)} %bitcast.28), calls=%async_computation.2 | async-start | bytes 6291456 | tf_op jit(solution)/shard_map/all_to_all | solution.py:77
  518.6 9.5 %copy-start.1 = (bf16[128,1024]{1,0:T(8,128)(2,1)S(1)}, bf16[128,1024]{1,0:T(8,128)(2,1)}, u32[]{:S(2)}) copy-start(bf16[128,1024]{1,0:T(8,128)(2,1)} %param.9) | copy-start | bytes 786436
Sparse Core Ops, SparseCore 0:
  9.4 128.0 all-gather.2
  143.7 29.5 reduce-scatter.1
  262.6 80.0 all-gather.4
